TPU v7x, 512 devices: a whole 4x4x16 slice. The times are simulated.
512 devices in a mesh: ops: 16 (over x, y), sec: 32 (over z, core).
Axes of the slice: x: 4, y: 4, z: 16, core: 2. Of those that a mesh axis runs over, the one named last changes fastest.
Arguments:
- wave: bfloat16 [32, 768, 768], P('sec')
- left_ops: bfloat16 [16, 32, 768, 768], P('ops', 'sec'), may hold values from -0.21875 to 0.21875
- right_ops: bfloat16 [16, 32, 768, 768], P('ops', 'sec'), may hold values from -0.21875 to 0.21875
- priors: bfloat16 [8, 32, 768, 768], P(None, 'sec', 'ops'), as said below
- row_sizes: int32 [32], P('sec'), may hold values from 64 to 768, as said below
- col_sizes: int32 [32], P('sec'), may hold values from 64 to 768, as said below
Outputs:
- sigma: bfloat16 [32, 768, 768], P('sec', 'ops')
- new_dir: bfloat16 [32, 768, 768], P('sec', 'ops')
- correlations: float32 [8], replicated
Inputs may be any that keep to these rules, and one draw needn't show every extreme that they name: `row_sizes`: one sector's block uses all 768 rows. `col_sizes`: one sector's block uses all 768 columns. `priors`: each prior vector has a norm of about one over all cells.
All inputs are finite; a program needn't handle non-finite values.
Results may differ from a plain program's by a relative error of at most 0.012.
Values sent between devices are 32-bit elements; how exact they have to be, the bound alone decides.
No kernel may reach another device: no remote copies, remote signals or barrier semaphores. Data moves between devices by JAX's collectives and lax.ppermute only.
A program may use at most 64 MiB of HBM per device.

v0:
```python
import jax
import jax.numpy as jnp
from jax import lax
from jax.sharding import PartitionSpec as P


def shards(wave, left_ops, right_ops, priors, row_sizes, col_sizes):
    width = wave.shape[1]
    sec_local = wave.shape[0]
    shard_rows = width // lax.axis_size("ops")
    first_row = lax.axis_index("ops") * shard_rows
    place = jnp.arange(width, dtype=jnp.int32)
    row_mask = (place[None, :] < row_sizes[:, None]).astype(jnp.float32)
    col_mask = (place[None, :] < col_sizes[:, None]).astype(jnp.float32)
    full_mask = row_mask[:, :, None] * col_mask[:, None, :]
    masked = wave * full_mask.astype(jnp.bfloat16)
    inner = jnp.einsum(
        "sab,ksjb->ksaj", masked, right_ops, preferred_element_type=jnp.float32
    ).astype(jnp.bfloat16)
    partial_all = jnp.einsum("ksia,ksaj->sij", left_ops, inner, preferred_element_type=jnp.float32)
    whole = lax.psum(partial_all, "ops")
    summed = lax.dynamic_slice_in_dim(whole, first_row, shard_rows, 1)
    mine_rows = lax.dynamic_slice_in_dim(row_mask, first_row, shard_rows, 1)
    mine_mask = mine_rows[:, :, None] * col_mask[:, None, :]
    sigma = (summed * mine_mask).astype(jnp.bfloat16)
    pmask = (priors * mine_mask[None].astype(jnp.bfloat16)).astype(jnp.float32)
    sig32 = sigma.astype(jnp.float32)
    local_over = jnp.einsum("psab,sab->p", pmask, sig32, precision=lax.Precision.HIGHEST)
    correlations = lax.psum(local_over, ("ops", "sec"))
    resid = sig32 - jnp.einsum("p,psab->sab", correlations, pmask, precision=lax.Precision.HIGHEST)
    total = lax.psum(jnp.sum(resid * resid), ("ops", "sec"))
    cells = sec_local * lax.axis_size("sec") * width * width
    new_dir = (resid / jnp.sqrt(total / cells + 1e-06)).astype(jnp.bfloat16)
    return (sigma, new_dir, correlations)


def solution(mesh):
    in_specs = (
        P("sec", None, None),
        P("ops", "sec", None, None),
        P("ops", "sec", None, None),
        P(None, "sec", "ops", None),
        P("sec"),
        P("sec"),
    )
    out_specs = (P("sec", "ops", None), P("sec", "ops", None), P())
    return jax.shard_map(shards, mesh=mesh, in_specs=in_specs, out_specs=out_specs, check_vma=False)
```

profile of v0, /device:TPU:1, one launch (start us, length us, event | category | flops | bytes accessed | tf_op | source)
XLA Modules:
  0.0 362.4 jit_solution(13174631265643082113)
XLA Ops:
  7.2 0.0 copy-start
  7.2 0.0 all-reduce.2.cloned.1.call-start
  8.6 0.0 copy-done
  8.6 5.6 %convolution_bitcast_fusion = f32[1,768,768]{1,2,0:T(8,128)} fusion(bf16[1,1,768,768]{3,2,1,0:T(8,128)(2,1)S(1)} %copy-done, bf16[1,768,768]{2,1,0:T(8,128)(2,1)} %param.6, bf16[1,1,768,768]{3,2,1,0:T(8,128)(2,1)} %param.8, f32[768]{0:T(1024)S(1)} %get-tuple-element.7, f32[768]{0:T(1024)S(1)} %get-tuple-element.6), kind=kOutput, calls=%fused_computation.1 | convolution fusion | flops 1814298624 | bytes 5904384 | tf_op jit(solution)/shard_map/ksia,ksaj->sij/dot_general | solution.py:20
  14.2 0.0 copy-start.1
  14.2 0.0 all-reduce.2.cloned.1.call-update
  14.2 0.1 multiply_convert_fusion.2
  14.3 0.9 copy-done.1
  15.3 125.8 %all-reduce.2.cloned.1.call-done = f32[1,768,768]{1,2,0:T(8,128)} async-done(((f32[1,768,768]{1,2,0:T(8,128)}), f32[1,768,768]{1,2,0:T(8,128)}) %all-reduce.2.cloned.1.call-update) | async-done | bytes 2359312 | tf_op jit(solution)/shard_map/psum | solution.py:21
  141.1 1.4 fusion.19
  142.5 0.2 copy.12
  142.7 0.5 convolution_bitcast_fusion.1
  143.2 105.0 %psum.22 = f32[8]{0:T(128)S(1)} all-reduce(f32[8]{0:T(128)S(1)} %convolution_bitcast_fusion.1), channel_id=1, replica_groups=mesh['ops'=16,'sec'=32] {'ops','sec'}, use_global_device_ids=true, to_apply=%region_1.0 | all-reduce | flops 8 | bytes 64 | tf_op jit(solution)/shard_map/psum | solution.py:29
  248.2 0.0 copy-start.2
  248.2 0.6 fusion.11
  248.8 0.2 copy.13
  249.0 1.4 multiply_convert_fusion.1
  250.4 2.0 multiply_reduce_fusion
  252.4 0.0 copy-done.2
  252.4 0.8 copy.9
  253.2 99.5 %psum.23 = f32[]{:T(128)} all-reduce(f32[]{:T(128)} %multiply_reduce_fusion), channel_id=1, replica_groups=mesh['ops'=16,'sec'=32] {'ops','sec'}, use_global_device_ids=true, to_apply=%region_3.0 | all-reduce | flops 1 | bytes 8 | tf_op jit(solution)/shard_map/psum | solution.py:31
  353.4 1.4 divide_convert_fusion
  354.8 0.8 copy.10
  (3 shorter events, 0.1 us)
Async XLA Ops:
  7.2 1.5 copy-start
  7.2 133.9 %all-reduce.2.cloned.1.call-start = ((), (), s32[]{:S(2)}) async-start(), calls=%async_computation | async-start | bytes 4718592 | tf_op jit(solution)/shard_map/psum | solution.py:21
  14.2 1.1 copy-start.1
  248.2 4.3 %copy-start.2 = (f32[8]{0:T(128)}, f32[8]{0:T(128)S(1)}, u32[]{:S(2)}) copy-start(f32[8]{0:T(128)S(1)} %psum.22) | copy-start | bytes 100
Sparse Core Ops, SparseCore 0:
  14.3 126.6 all-reduce.1
where the time goes:
time: 363 us; the launch traced here: 362 us
  blocking collectives  204 us (56%)
  waiting for transfers between devices  126 us (35%)
  between operations  16.2 us (4%)
  matrix products  6.72 us (2%)
  other arithmetic  6.38 us (2%)
    psum x1, waiting for transfers between devices, shards(): whole = lax.psum(partial_all, 'ops')  126 us
    psum x1, blocking collectives, shards(): correlations = lax.psum(local_over, ('ops', 'sec'))  105 us
    psum x1, blocking collectives, shards(): total = lax.psum(jnp.sum(resid * resid), ('ops', 'sec'))  99.5 us
  transfers between devices with their start and end apart: 1, of which 1 were waited for; matrix products, arithmetic and copies ran while one was open for 0% of the time, Pallas kernels for 0%

commit v1 on v0

--- a/solution.py
+++ b/solution.py
@@ -2,6 +2,7 @@
 import jax.numpy as jnp
 from jax import lax
 from jax.sharding import PartitionSpec as P
+from jax.lax import all_gather
 
 
 def shards(wave, left_ops, right_ops, priors, row_sizes, col_sizes):
@@ -18,7 +19,12 @@
         "sab,ksjb->ksaj", masked, right_ops, preferred_element_type=jnp.float32
     ).astype(jnp.bfloat16)
     partial_all = jnp.einsum("ksia,ksaj->sij", left_ops, inner, preferred_element_type=jnp.float32)
-    whole = lax.psum(partial_all, "ops")
+
+    def set_roads(base_x):
+        tall = jnp.sum(all_gather(base_x, "ops"), axis=0)
+        return tall
+
+    whole = set_roads(partial_all)
     summed = lax.dynamic_slice_in_dim(whole, first_row, shard_rows, 1)
     mine_rows = lax.dynamic_slice_in_dim(row_mask, first_row, shard_rows, 1)
     mine_mask = mine_rows[:, :, None] * col_mask[:, None, :]

time: 363 us -> 510 us (1.40)
  waiting for transfers between devices: 126 us -> 239 us
  local copies, waits for them, and re-layouts: 2.84 us -> 24.1 us
  other arithmetic: 6.38 us -> 18.5 us
    all_gather x0 -> x1, waiting for transfers between devices: none -> 239 us  [set_roads(): tall = jnp.sum(all_gather(base_x, 'ops'), axis=0)]
    psum x1 -> x0, waiting for transfers between devices: 126 us -> none  [shards(): whole = lax.psum(partial_all, 'ops')]
    unnamed x8 -> x11, local copies, waits for them, and re-layouts: 2.47 us -> 23.6 us
    reduce_sum x0 -> x1, other arithmetic: none -> 16.2 us  [set_roads(): tall = jnp.sum(all_gather(base_x, 'ops'), axis=0)]
where the time goes in v1:
time: 510 us; the launch traced here: 509 us
  waiting for transfers between devices  239 us (47%)
  blocking collectives  204 us (40%)
  local copies, waits for them, and re-layouts  24.1 us (5%)
  other arithmetic  18.5 us (4%)
  between operations  16.2 us (3%)
  matrix products  6.73 us (1%)
    all_gather x1, waiting for transfers between devices, set_roads(): tall = jnp.sum(all_gather(base_x, 'ops'), axis=0)  239 us
    psum x1, blocking collectives, shards(): correlations = lax.psum(local_over, ('ops', 'sec'))  104 us
    psum x1, blocking collectives, shards(): total = lax.psum(jnp.sum(resid * resid), ('ops', 'sec'))  100 us
    unnamed x11, local copies, waits for them, and re-layouts  23.6 us
    reduce_sum x1, other arithmetic, set_roads(): tall = jnp.sum(all_gather(base_x, 'ops'), axis=0)  16.2 us
  transfers between devices with their start and end apart: 1, of which 1 were waited for; matrix products, arithmetic and copies ran while one was open for 0% of the time, Pallas kernels for 0%

profile of v1, /device:TPU:1, one launch (start us, length us, event | category | flops | bytes accessed | tf_op | source)
XLA Modules:
  0.0 509.0 jit_solution(15737355565459272287)
XLA Ops:
  7.2 0.0 copy-start
  7.2 0.0 all-gather.3.cloned.1.call-start
  8.6 0.0 copy-done
  8.6 5.6 %convolution_bitcast_fusion = f32[768,768]{0,1:T(8,128)} fusion(bf16[1,1,768,768]{3,2,1,0:T(8,128)(2,1)S(1)} %copy-done, bf16[1,768,768]{2,1,0:T(8,128)(2,1)} %param.6, bf16[1,1,768,768]{3,2,1,0:T(8,128)(2,1)} %param.8, f32[768]{0:T(1024)S(1)} %get-tuple-element.9, f32[768]{0:T(1024)S(1)} %get-tuple-element.8), kind=kOutput, calls=%fused_computation.2 | convolution fusion | flops 1814298624 | bytes 5904384 | tf_op jit(solution)/shard_map/ksia,ksaj->sij/dot_general | solution.py:21
  14.2 0.0 all-gather.3.cloned.1.call-update
  14.2 239.0 %all-gather.3.cloned.1.call-done = f32[12288,768]{0,1:T(8,128)} async-done(((f32[768,768]{0,1:T(8,128)}), f32[12288,768]{0,1:T(8,128)}) %all-gather.3.cloned.1.call-update) | async-done | bytes 37748752 | tf_op jit(solution)/shard_map/all_gather | solution.py:24
  253.2 22.0 %copy.15 = f32[96,8,16,768]{3,2,1,0:T(8,128)S(1)} copy(f32[96,8,16,768]{3,1,2,0:T(8,128)} %bitcast.54) | data formatting | bytes 75497472
  275.3 16.2 %bitcast_reduce_fusion = f32[768,768]{0,1:T(8,128)} fusion(f32[96,8,16,768]{3,2,1,0:T(8,128)S(1)} %copy.15), kind=kLoop, calls=%fused_computation | loop fusion | flops 8847360 | bytes 40108032 | tf_op jit(solution)/shard_map/reduce_sum | solution.py:24
  291.5 0.0 copy-start.2
  291.5 1.5 multiply_convert_fusion.1
  292.9 0.1 copy.9
  293.1 0.2 copy.13
  293.3 0.0 copy-done.2
  293.3 0.5 convolution_bitcast_fusion.1
  293.9 104.2 %psum.14 = f32[8]{0:T(128)S(1)} all-reduce(f32[8]{0:T(128)S(1)} %convolution_bitcast_fusion.1), channel_id=1, replica_groups=mesh['ops'=16,'sec'=32] {'ops','sec'}, use_global_device_ids=true, to_apply=%region_1.0 | all-reduce | flops 8 | bytes 64 | tf_op jit(solution)/shard_map/psum | solution.py:35
  398.0 0.0 copy-start.3
  398.0 0.0 copy-start.1
  398.0 0.6 fusion.11
  398.7 0.2 copy.14
  398.9 0.7 multiply_reduce_fusion
  399.6 0.8 copy.10
  400.3 100.3 %psum.15 = f32[]{:T(128)} all-reduce(f32[]{:T(128)} %multiply_reduce_fusion), channel_id=1, replica_groups=mesh['ops'=16,'sec'=32] {'ops','sec'}, use_global_device_ids=true, to_apply=%region_3.0 | all-reduce | flops 1 | bytes 8 | tf_op jit(solution)/shard_map/psum | solution.py:37
  501.3 0.1 fusion.15
  501.4 0.0 copy-done.3
  501.4 0.8 copy.11
  502.2 0.0 copy-done.1
  (3 shorter events, 0.1 us)
Async XLA Ops:
  7.2 1.5 copy-start
  7.2 246.1 %all-gather.3.cloned.1.call-start = ((), (), s32[]{:S(2)}) async-start(), calls=%async_computation | async-start | bytes 40108032 | tf_op jit(solution)/shard_map/all_gather | solution.py:24
  291.5 1.8 copy-start.2
  398.0 103.4 %copy-start.3 = (f32[8]{0:T(128)}, f32[8]{0:T(128)S(1)}, u32[]{:S(2)}) copy-start(f32[8]{0:T(128)S(1)} %psum.14) | copy-start | bytes 100
  398.0 104.2 %copy-start.1 = (bf16[1,1,768,768]{3,2,1,0:T(8,128)(2,1)S(1)}, bf16[1,1,768,768]{3,2,1,0:T(8,128)(2,1)}, u32[]{:S(2)}) copy-start(bf16[1,1,768,768]{3,2,1,0:T(8,128)(2,1)} %param.7) | copy-start | bytes 3538948
Sparse Core Ops, SparseCore 0:
  14.3 238.8 all-gather.2
